TPU v7x, 32 devices: a whole 2x2x4 slice. The times are simulated.
32 devices in a mesh: pole: 2 (over x), row: 8 (over z, y), col: 2 (over core).
Axes of the slice: x: 2, y: 2, z: 4, core: 2. Of those that a mesh axis runs over, the one named last changes fastest.
Arguments:
- anc_inverse: bfloat16 [2048, 1024], P(('pole', 'row')), parts along dimension 0, as said below
- parent_pivinv: float32 [2048, 1024], P(('pole', 'row')), parts along dimension 0, as said below
- parent_lower: bfloat16 [2048, 1024], P(('pole', 'row')), parts along dimension 0, may hold values from -0.1875 to 0.1875
- parent_mask: int32 [4], replicated, may hold values 0 or 1
- leaf_lower_par: bfloat16 [2048, 1024], P(('pole', 'row')), parts along dimension 0, may hold values from -0.125 to 0.125
- leaf_lower_anc: bfloat16 [2048, 1024], P(('pole', 'row')), parts along dimension 0, may hold values from -0.125 to 0.125
- leaf_mask: int32 [8], replicated, may hold values 0 or 1
- leaf_pivots: float32 [2048], P(('pole', 'col')), parts along dimension 0, may hold values from 0.5 to 2
Outputs:
- parent_block: float32 [2048, 1024], P(('pole', 'row')), parts along dimension 0
- parent_offdiag: bfloat16 [2048, 1024], P(('pole', 'row'), 'col'), parts along dimension 0
- leaf_par_block: bfloat16 [2048, 1024], P(('pole', 'row'), 'col'), parts along dimension 0
- leaf_anc_block: bfloat16 [2048, 1024], P(('pole', 'row'), 'col'), parts along dimension 0
- density: float32 [2048], P(('pole', 'col')), parts along dimension 0
There are 2 independent parts, one for each index of `pole`. A program takes and returns all parts, laid end to end along the dimension named above; an argument that names none is the same for every part. Nothing has to cross between parts.
Inputs may be any that keep to these rules, and one draw needn't show every extreme that they name: `anc_inverse`: symmetric. `parent_pivinv`: symmetric. `parent_mask`: 1 marks a structurally nonzero block of 256 rows. `leaf_mask`: 1 marks a structurally nonzero block of 256 rows.
All inputs are finite; a program needn't handle non-finite values.
Results may differ from a plain program's by a relative error of at most 0.0095.
Values may be sent and summed in bfloat16 or wider, within the bound.
No kernel may reach another device: no remote copies, remote signals or barrier semaphores. Data moves between devices by JAX's collectives and lax.ppermute only.
A program may use at most 64 MiB of HBM per device.

v0:
```python
import jax
import jax.numpy as jnp
from jax import lax
from jax.sharding import PartitionSpec as P

BLOCK = 256
ORDER = 1024


def local(
    anc_inverse,
    parent_pivinv,
    parent_lower,
    parent_mask,
    leaf_lower_par,
    leaf_lower_anc,
    leaf_mask,
    leaf_pivots,
):
    row_index = lax.axis_index("row")
    row_devices = lax.axis_size("row")
    col_index = lax.axis_index("col")
    anc_rows = anc_inverse.shape[0]
    order_rows = parent_pivinv.shape[0]
    col_width = leaf_pivots.shape[0]
    parent_gate = lax.dynamic_slice_in_dim(
        jnp.repeat(parent_mask, BLOCK), row_index * anc_rows, anc_rows
    )
    lower_one = parent_lower * parent_gate[:, None].astype(jnp.bfloat16)
    lower_half = lax.dynamic_slice_in_dim(lower_one, col_index * col_width, col_width, 1)
    leaf_gate = jnp.repeat(leaf_mask, BLOCK)
    gate_par = lax.dynamic_slice_in_dim(leaf_gate[:ORDER], row_index * order_rows, order_rows)
    gate_anc = lax.dynamic_slice_in_dim(leaf_gate[ORDER:], row_index * anc_rows, anc_rows)
    leaf_local = jnp.concatenate(
        [
            leaf_lower_par * gate_par[:, None].astype(jnp.bfloat16),
            leaf_lower_anc * gate_anc[:, None].astype(jnp.bfloat16),
        ],
        axis=0,
    )
    leaf_half = lax.dynamic_slice_in_dim(leaf_local, col_index * col_width, col_width, 1)
    columns = anc_inverse
    product = jnp.dot(
        columns,
        lax.all_gather(lower_half, "row", axis=0, tiled=True),
        preferred_element_type=jnp.float32,
    )
    parent_offdiag = (-product).astype(jnp.bfloat16)
    offdiag_rows = lax.all_gather(parent_offdiag, "col", axis=1, tiled=True)
    columns = lower_one
    diag_sums = lax.psum_scatter(
        lax.dot_general(
            columns, offdiag_rows, (((0,), (0,)), ((), ())), preferred_element_type=jnp.float32
        ),
        "row",
        scatter_dimension=0,
        tiled=True,
    )
    parent_block = parent_pivinv - diag_sums
    parent_round = parent_block.astype(jnp.bfloat16)
    mirrored = lax.all_to_all(offdiag_rows, "row", split_axis=1, concat_axis=0, tiled=True).T
    upper_rows = jnp.concatenate(
        [
            parent_round.reshape(order_rows, row_devices, order_rows),
            mirrored.reshape(order_rows, row_devices, anc_rows),
        ],
        axis=2,
    )
    lower_rows = jnp.concatenate(
        [
            offdiag_rows.reshape(anc_rows, row_devices, order_rows),
            anc_inverse.reshape(anc_rows, row_devices, anc_rows),
        ],
        axis=2,
    )
    inverse_rows = jnp.concatenate(
        [upper_rows.reshape(order_rows, -1), lower_rows.reshape(anc_rows, -1)], axis=0
    )
    columns = inverse_rows
    leaf_product = jnp.dot(
        columns,
        lax.all_gather(leaf_half, "row", axis=0, tiled=True),
        preferred_element_type=jnp.float32,
    )
    leaf_result = (-leaf_product).astype(jnp.bfloat16)
    partial_sums = jnp.sum(leaf_half.astype(jnp.float32) * leaf_result.astype(jnp.float32), axis=0)
    density = leaf_pivots - lax.psum(partial_sums, "row")
    return (
        parent_block,
        parent_offdiag,
        leaf_result[:order_rows],
        leaf_result[order_rows:],
        density,
    )


def solution(mesh):
    placed = (
        P(("pole", "row"), None),
        P(("pole", "row"), None),
        P(("pole", "row"), None),
        P(),
        P(("pole", "row"), None),
        P(("pole", "row"), None),
        P(),
        P(("pole", "col")),
    )
    return jax.shard_map(
        local,
        mesh=mesh,
        in_specs=placed,
        out_specs=(
            P(("pole", "row"), None),
            P(("pole", "row"), "col"),
            P(("pole", "row"), "col"),
            P(("pole", "row"), "col"),
            P(("pole", "col")),
        ),
        check_vma=False,
    )
```

profile of v0, /device:TPU:0, one launch (start us, length us, event | category | flops | bytes accessed | tf_op | source)
XLA Modules:
  0.0 232.6 jit_solution(13250326127232926921)
XLA Ops:
  7.2 0.0 copy-start
  7.2 0.0 all-gather.3.cloned.1.call-start
  7.2 0.6 copy-done
  7.8 0.1 broadcast_bitcast_fusion.2
  7.9 0.1 dynamic-slice_convert_fusion.2
  8.0 1.0 broadcast_multiply_fusion.2
  9.0 0.7 constant_dynamic-slice_fusion
  9.7 0.0 all-gather.3.cloned.1.call-update
  9.7 0.0 reduce-scatter.2.cloned.1.call-start
  9.8 43.8 %all-gather.3.cloned.1.call-done = bf16[1024,512]{1,0:T(8,128)(2,1)} async-done(((bf16[128,512]{1,0:T(8,128)(2,1)}), bf16[1024,512]{1,0:T(8,128)(2,1)}) %all-gather.3.cloned.1.call-update) | async-done | bytes 1048592 | tf_op jit(solution)/shard_map/all_gather | solution.py:45
  53.6 1.7 fusion.2
  55.3 2.0 all_gather.10
  57.3 2.7 %fusion.10 = f32[1024,1024]{1,0:T(8,128)} fusion(bf16[128,1024]{1,0:T(8,128)(2,1)S(1)} %broadcast_multiply_fusion.2, bf16[128,1024]{0,1:T(8,128)(2,1)S(1)} %all_gather.10), kind=kOutput, calls=%fused_computation.28 | convolution fusion | flops 268435456 | bytes 4718592 | tf_op jit(solution)/shard_map/dot_general | solution.py:52
  60.0 0.0 reduce-scatter.2.cloned.1.call-update
  60.1 0.0 copy-start.1
  60.1 0.0 all-gather.5.cloned.1.call-start
  60.1 0.6 copy-done.7
  60.7 0.1 fusion.9
  60.8 0.1 broadcast_bitcast_fusion.1
  60.8 0.1 broadcast_bitcast_fusion
  60.9 0.1 dynamic-slice_convert_fusion
  61.0 0.0 copy-done.4
  61.0 0.1 broadcast_multiply_fusion
  61.1 0.0 copy-done.5
  61.1 0.1 broadcast_multiply_fusion.1
  61.2 0.0 copy-start.3
  61.2 0.7 fusion.6
  62.0 0.0 all-gather.5.cloned.1.call-update
  62.0 0.9 copy.16
  62.8 3.4 %all-to-all-start = ((bf16[128,8,128]{2,0,1:T(8,128)(2,1)}), bf16[128,8,128]{2,0,1:T(8,128)(2,1)S(1)}, u32[]{:S(2)}, u32[]{:S(2)}) async-start(bf16[128,8,128]{2,0,1:T(8,128)(2,1)} %copy.16), calls=%async_computation.1 | async-start | bytes 524288 | tf_op jit(solution)/shard_map/all_to_all | solution.py:61
  66.3 0.0 copy-done.1
  66.3 0.2 copy.22
  66.4 0.8 copy.20
  67.3 15.4 %all-to-all-done = bf16[128,8,128]{2,0,1:T(8,128)(2,1)S(1)} async-done(((bf16[128,8,128]{2,0,1:T(8,128)(2,1)}), bf16[128,8,128]{2,0,1:T(8,128)(2,1)S(1)}, u32[]{:S(2)}, u32[]{:S(2)}) %all-to-all-start) | async-done | bytes 262176 | tf_op jit(solution)/shard_map/all_to_all | solution.py:61
  82.7 0.2 copy.17
  82.9 0.0 copy-start.2
  82.9 69.2 %reduce-scatter.2.cloned.1.call-done = f32[128,1024]{1,0:T(8,128)} async-done(((f32[1024,1024]{1,0:T(8,128)}), f32[128,1024]{1,0:T(8,128)}) %reduce-scatter.2.cloned.1.call-update) | async-done | bytes 524304 | tf_op jit(solution)/shard_map/reduce_scatter | solution.py:51
  152.1 0.0 copy-done.3
  152.1 2.0 convert_bitcast_fusion
  154.1 0.1 pad_maximum_fusion
  154.2 0.4 copy.21
  154.6 48.9 %all-gather.5.cloned.1.call-done = bf16[2048,512]{1,0:T(8,128)(2,1)} async-done(((bf16[256,512]{1,0:T(8,128)(2,1)}), bf16[2048,512]{1,0:T(8,128)(2,1)}) %all-gather.5.cloned.1.call-update) | async-done | bytes 2097168 | tf_op jit(solution)/shard_map/all_gather | solution.py:82
  203.5 0.0 copy-done.2
  203.5 2.4 %multiply_reduce_fusion = (f32[512]{0:T(512)S(1)}, bf16[256,512]{1,0:T(8,128)(2,1)S(1)}) fusion(bf16[256,512]{1,0:T(8,128)(2,1)S(1)} %copy-done.2, bf16[2048,512]{1,0:T(8,128)(2,1)} %all-gather.5.cloned.1.call-done, bf16[128,2048]{0,1:T(8,128)(2,1)S(1)} %bitcast.35, bf16[128,2048]{0,1:T(8,128)(2,1)S(1)} %bitcast.36), kind=kOutput, calls=%fused_computation.12 | convolution fusion | flops 539753984 | bytes 3672064 | tf_op jit(solution)/shard_map/dot_general | solution.py:80
  205.9 0.7 fusion.8
  206.6 18.9 %psum.7 = f32[512]{0:T(512)S(1)} all-reduce(f32[512]{0:T(512)S(1)} %get-tuple-element.21), channel_id=1, replica_groups=mesh['pole'=2,'row'=8,'col'=2] {'row'}, use_global_device_ids=true, to_apply=%region_2.0 | all-reduce | flops 512 | bytes 4096 | tf_op jit(solution)/shard_map/psum | solution.py:87
  225.5 0.0 copy-done.6
  225.5 0.6 sub.7
  (9 shorter events, 0.1 us)
Async XLA Ops:
  7.2 0.7 copy-start
  7.2 46.4 %all-gather.3.cloned.1.call-start = ((), (), s32[]{:S(2)}) async-start(), calls=%async_computation.2 | async-start | bytes 1179648 | tf_op jit(solution)/shard_map/all_gather | solution.py:45
  9.7 142.3 %reduce-scatter.2.cloned.1.call-start = ((), (), s32[]{:S(2)}) async-start(), calls=%async_computation.3 | async-start | bytes 4718592 | tf_op jit(solution)/shard_map/reduce_scatter | solution.py:51
  60.0 0.7 copy-start.7
  60.0 1.0 copy-start.4
  60.0 1.1 copy-start.5
  60.1 6.2 %copy-start.1 = (bf16[128,1024]{1,0:T(8,128)(2,1)S(1)}, bf16[128,1024]{1,0:T(8,128)(2,1)}, u32[]{:S(2)}) copy-start(bf16[128,1024]{1,0:T(8,128)(2,1)} %param.8) | copy-start | bytes 786436
  60.1 143.4 %all-gather.5.cloned.1.call-start = ((), (), s32[]{:S(2)}) async-start(), calls=%async_computation.4 | async-start | bytes 2359296 | tf_op jit(solution)/shard_map/all_gather | solution.py:82
  61.2 90.9 %copy-start.3 = (f32[128,1024]{1,0:T(8,128)S(1)}, f32[128,1024]{1,0:T(8,128)}, u32[]{:S(2)}) copy-start(f32[128,1024]{1,0:T(8,128)} %param.9) | copy-start | bytes 1572868
  62.8 19.9 %all-to-all-start = ((bf16[128,8,128]{2,0,1:T(8,128)(2,1)}), bf16[128,8,128]{2,0,1:T(8,128)(2,1)S(1)}, u32[]{:S(2)}, u32[]{:S(2)}) async-start(bf16[128,8,128]{2,0,1:T(8,128)(2,1)} %copy.16), calls=%async_computation.1 | async-start | bytes 524288 | tf_op jit(solution)/shard_map/all_to_all | solution.py:61
  82.9 120.6 %copy-start.2 = (bf16[256,512]{1,0:T(8,128)(2,1)S(1)}, bf16[256,512]{1,0:T(8,128)(2,1)}, u32[]{:S(2)}) copy-start(bf16[256,512]{1,0:T(8,128)(2,1)} %fusion.6) | copy-start | bytes 786436
  203.5 22.0 %copy-start.6 = (f32[512]{0:T(512)S(1)}, f32[512]{0:T(512)}, u32[]{:S(2)}) copy-start(f32[512]{0:T(512)} %param.15) | copy-start | bytes 6148
Sparse Core Ops, SparseCore 0:
  10.7 42.8 all-gather.2
  60.2 91.8 reduce-scatter.1
  154.4 49.0 all-gather.4
where the time goes:
time: 233 us
  waiting for transfers between devices  177 us (76%)
  blocking collectives  20.9 us (9%)
  between operations  13.9 us (6%)
  matrix products  6.8 us (3%)
  local copies, waits for them, and re-layouts  5.36 us (2%)
  other arithmetic  4.75 us (2%)
  starting transfers between devices  3.53 us (2%)
    reduce_scatter x1, waiting for transfers between devices, local(): lax.psum_scatter(lax.dot_general(columns, offdiag_rows, (((0,), (0,)), ((...  69.2 us
    all_gather x1, waiting for transfers between devices, local(): lax.all_gather(leaf_half, 'row', axis=0, tiled=True)  48.9 us
    all_gather x1, waiting for transfers between devices, local(): lax.all_gather(lower_half, 'row', axis=0, tiled=True)  43.8 us
    psum x1, blocking collectives, local(): density = leaf_pivots - lax.psum(partial_sums, 'row')  18.9 us
    all_to_all x1, waiting for transfers between devices, local(): lax.all_to_all(offdiag_rows, 'row', split_axis=1, concat_axis=0, tiled=True)  15.4 us
  transfers between devices with their start and end apart: 4, of which 4 were waited for; matrix products, arithmetic and copies ran while one was open for 2% of the time, Pallas kernels for 0%

commit v1 on v0

--- a/solution.py
+++ b/solution.py
@@ -5,6 +5,32 @@
 
 BLOCK = 256
 ORDER = 1024
+
+
+def guide_samples(matrix, d_out):
+    reply = list(matrix.shape[1:])
+    reply[d_out] *= matrix.shape[0]
+    parts_out = jnp.moveaxis(matrix, 0, d_out).reshape(reply)
+    return parts_out
+
+
+def _time_racks(mat, axis_key, k_dim):
+    nd = lax.axis_size(axis_key)
+    xs_all = [(no, (no + 1) % nd) for no in range(nd)]
+    e_now, now = ([], [])
+    c = 0
+    vals = [(t, dev) for dev, t in xs_all]
+    while c < nd - 1:
+        if c % 2 == 0:
+            e_now.append(lax.ppermute(e_now[-1] if e_now else mat, axis_key, perm=xs_all))
+        else:
+            now.append(lax.ppermute(now[-1] if now else mat, axis_key, vals))
+        c = c + 1
+    current_arr = jnp.stack([*e_now[::-1], mat, *now], axis=0)
+    right_arr = lax.axis_index(axis_key) - len(e_now)
+    current_arr = current_arr[(jnp.arange(nd) - right_arr) % nd]
+    formed = guide_samples(current_arr, k_dim)
+    return formed
 
 
 def local(
@@ -78,9 +104,7 @@
     )
     columns = inverse_rows
     leaf_product = jnp.dot(
-        columns,
-        lax.all_gather(leaf_half, "row", axis=0, tiled=True),
-        preferred_element_type=jnp.float32,
+        columns, _time_racks(leaf_half, "row", 0), preferred_element_type=jnp.float32
     )
     leaf_result = (-leaf_product).astype(jnp.bfloat16)
     partial_sums = jnp.sum(leaf_half.astype(jnp.float32) * leaf_result.astype(jnp.float32), axis=0)

time: 233 us -> 202 us (0.87)
  waiting for transfers between devices: 177 us -> 118 us
  starting transfers between devices: 3.53 us -> 23 us
  local copies, waits for them, and re-layouts: 5.36 us -> 13.2 us
    all_gather x1 -> x0, waiting for transfers between devices: 48.9 us -> none  [local(): lax.all_gather(leaf_half, 'row', axis=0, tiled=True)]
    ppermute x0 -> x7, waiting for transfers between devices: none -> 46.9 us  [the longest x4 46.8 us: _time_racks(): lax.ppermute(e_now[-1] if e_now else mat, axis_key, perm=xs_all)]
    reduce_scatter x1, waiting for transfers between devices: 69.2 us -> 24.7 us  [local(): lax.psum_scatter(lax.dot_general(columns, offdiag_rows, (((0,), (0,)), ((...]
    ppermute x0 -> x7, starting transfers between devices: none -> 14.7 us  [the longest x3 14 us: _time_racks(): now.append(lax.ppermute(now[-1] if now else mat, axis_key, vals))]
    all_to_all x1, waiting for transfers between devices: 15.4 us -> 2.65 us  [local(): lax.all_to_all(offdiag_rows, 'row', split_axis=1, concat_axis=0, tiled=True)]
    all_to_all x1, starting transfers between devices: 3.41 us -> 8.19 us  [local(): lax.all_to_all(offdiag_rows, 'row', split_axis=1, concat_axis=0, tiled=True)]
    unnamed x24 -> x39, local copies, waits for them, and re-layouts: 2.25 us -> 6.28 us
  transfers between devices with their start and end apart: 4 -> 10, of which waited for: 4 -> 8; matrix products, arithmetic and copies ran while one was open for 2% -> 5% of each run, Pallas kernels for 0% -> 0%
where the time goes in v1:
time: 202 us
  waiting for transfers between devices  118 us (58%)
  starting transfers between devices  23 us (11%)
  blocking collectives  22.2 us (11%)
  between operations  14.2 us (7%)
  local copies, waits for them, and re-layouts  13.2 us (7%)
  matrix products  6.39 us (3%)
  other arithmetic  4.85 us (2%)
    ppermute x4, waiting for transfers between devices, _time_racks(): lax.ppermute(e_now[-1] if e_now else mat, axis_key, perm=xs_all)  46.8 us
    all_gather x1, waiting for transfers between devices, local(): lax.all_gather(lower_half, 'row', axis=0, tiled=True)  43.8 us
    reduce_scatter x1, waiting for transfers between devices, local(): lax.psum_scatter(lax.dot_general(columns, offdiag_rows, (((0,), (0,)), ((...  24.7 us
    psum x1, blocking collectives, local(): density = leaf_pivots - lax.psum(partial_sums, 'row')  20.2 us
    ppermute x3, starting transfers between devices, _time_racks(): now.append(lax.ppermute(now[-1] if now else mat, axis_key, vals))  14 us
    all_to_all x1, starting transfers between devices, local(): lax.all_to_all(offdiag_rows, 'row', split_axis=1, concat_axis=0, tiled=True)  8.19 us
    unnamed x39, local copies, waits for them, and re-layouts  6.28 us
  transfers between devices with their start and end apart: 10, of which 8 were waited for; matrix products, arithmetic and copies ran while one was open for 5% of the time, Pallas kernels for 0%

profile of v1, /device:TPU:0, one launch (start us, length us, event | category | flops | bytes accessed | tf_op | source)
XLA Modules:
  0.0 201.9 jit_solution(11765824256758524244)
XLA Ops:
  7.2 0.6 copy-done
  7.8 0.1 broadcast_bitcast_fusion.2
  7.9 0.1 dynamic-slice_convert_fusion.2
  8.0 1.0 broadcast_multiply_fusion.2
  9.0 0.7 constant_dynamic-slice_fusion
  9.7 0.0 reduce-scatter.2.cloned.1.call-start
  9.8 43.8 %all-gather.2.cloned.1.call-done = bf16[1024,512]{1,0:T(8,128)(2,1)} async-done(((bf16[128,512]{1,0:T(8,128)(2,1)}), bf16[1024,512]{1,0:T(8,128)(2,1)}) %all-gather.2.cloned.1.call-update) | async-done | bytes 1048592 | tf_op jit(solution)/shard_map/all_gather | solution.py:71
  53.6 1.7 fusion.2
  55.3 2.0 all_gather.7
  57.3 2.7 %fusion.12 = f32[1024,1024]{1,0:T(8,128)} fusion(bf16[128,1024]{1,0:T(8,128)(2,1)S(1)} %broadcast_multiply_fusion.2, bf16[128,1024]{0,1:T(8,128)(2,1)S(1)} %all_gather.7), kind=kOutput, calls=%fused_computation.44 | convolution fusion | flops 268435456 | bytes 4718592 | tf_op jit(solution)/shard_map/dot_general | solution.py:78
  60.0 0.6 copy-done.11
  60.7 0.1 fusion.11
  60.7 0.1 broadcast_bitcast_fusion
  60.8 0.1 broadcast_bitcast_fusion.1
  60.9 0.1 dynamic-slice_convert_fusion
  61.0 0.1 broadcast_multiply_fusion.1
  61.1 0.1 broadcast_multiply_fusion
  61.2 0.6 collective-permute-start
  61.8 12.7 %collective-permute-done = bf16[256,512]{1,0:T(8,128)(2,1)S(1)} collective-permute-done((bf16[256,512]{1,0:T(8,128)(2,1)S(1)}, bf16[256,512]{1,0:T(8,128)(2,1)S(1)}, u32[]{:S(2)}, u32[]{:S(2)}) %collective-permute-start) | collective-permute-done | bytes 262176 | tf_op jit(solution)/shard_map/ppermute | solution.py:25
  74.5 4.7 %collective-permute-start.4 = (bf16[256,512]{1,0:T(8,128)(2,1)S(1)}, bf16[256,512]{1,0:T(8,128)(2,1)S(1)}, u32[]{:S(2)}, u32[]{:S(2)}) collective-permute-start(bf16[256,512]{1,0:T(8,128)(2,1)S(1)} %fusion.6), channel_id=1, source_target_pairs={{2,0},{4,2},{6,4},{8,6},{10,8},{12,10},{14,12},{0,14},{3,1},{5,3},... | collective-permute-start | bytes 786440 | tf_op jit(solution)/shard_map/ppermute | solution.py:27
  79.2 11.8 %collective-permute-done.1 = bf16[256,512]{1,0:T(8,128)(2,1)S(1)} collective-permute-done((bf16[256,512]{1,0:T(8,128)(2,1)S(1)}, bf16[256,512]{1,0:T(8,128)(2,1)S(1)}, u32[]{:S(2)}, u32[]{:S(2)}) %collective-permute-start.1) | collective-permute-done | bytes 262176 | tf_op jit(solution)/shard_map/ppermute | solution.py:25
  91.1 4.7 %collective-permute-start.5 = (bf16[256,512]{1,0:T(8,128)(2,1)S(1)}, bf16[256,512]{1,0:T(8,128)(2,1)}, u32[]{:S(2)}, u32[]{:S(2)}) collective-permute-start(bf16[256,512]{1,0:T(8,128)(2,1)S(1)} %collective-permute-done.4), channel_id=1, source_target_pairs={{2,0},{4,2},{6,4},{8,6},{10,8},{12,10},{14,12},{0,14},{3,1},{5,3},... | collective-permute-start | bytes 786440 | tf_op jit(solution)/shard_map/ppermute | solution.py:27
  95.8 11.4 %collective-permute-done.2 = bf16[256,512]{1,0:T(8,128)(2,1)S(1)} collective-permute-done((bf16[256,512]{1,0:T(8,128)(2,1)S(1)}, bf16[256,512]{1,0:T(8,128)(2,1)S(1)}, u32[]{:S(2)}, u32[]{:S(2)}) %collective-permute-start.2) | collective-permute-done | bytes 262176 | tf_op jit(solution)/shard_map/ppermute | solution.py:25
  107.2 0.0 collective-permute-start.3
  107.2 0.2 copy.22
  107.4 0.1 collective-permute-done.5
  107.6 4.6 %collective-permute-start.6 = (bf16[256,512]{1,0:T(8,128)(2,1)}, bf16[256,512]{1,0:T(8,128)(2,1)}, u32[]{:S(2)}, u32[]{:S(2)}) collective-permute-start(bf16[256,512]{1,0:T(8,128)(2,1)} %collective-permute-done.5), channel_id=1, source_target_pairs={{2,0},{4,2},{6,4},{8,6},{10,8},{12,10},{14,12},{0,14},{3,1},{5,3},... | collective-permute-start | bytes 786440 | tf_op jit(solution)/shard_map/ppermute | solution.py:27
  112.2 10.9 %collective-permute-done.3 = bf16[256,512]{1,0:T(8,128)(2,1)} collective-permute-done((bf16[256,512]{1,0:T(8,128)(2,1)S(1)}, bf16[256,512]{1,0:T(8,128)(2,1)}, u32[]{:S(2)}, u32[]{:S(2)}) %collective-permute-start.3) | collective-permute-done | bytes 262176 | tf_op jit(solution)/shard_map/ppermute | solution.py:25
  123.1 1.0 bitcast_dynamic-update-slice_fusion.7
  124.1 1.0 bitcast_dynamic-update-slice_fusion.6
  125.1 1.0 bitcast_dynamic-update-slice_fusion.5
  126.1 0.9 copy.16
  127.0 8.2 %all-to-all-start = ((bf16[128,8,128]{2,0,1:T(8,128)(2,1)}), bf16[128,8,128]{2,0,1:T(8,128)(2,1)S(1)}, u32[]{:S(2)}, u32[]{:S(2)}) async-start(bf16[128,8,128]{2,0,1:T(8,128)(2,1)} %copy.16), calls=%async_computation.1 | async-start | bytes 524288 | tf_op jit(solution)/shard_map/all_to_all | solution.py:87
  135.2 1.0 bitcast_dynamic-update-slice_fusion.1
  136.2 1.0 bitcast_dynamic-update-slice_fusion
  137.1 2.0 %gather_fusion = bf16[8,256,512]{2,1,0:T(8,128)(2,1)} fusion(bf16[8,256,512]{2,1,0:T(8,128)(2,1)S(1)} %bitcast_dynamic-update-slice_fusion, s32[1024]{0:T(1024)S(1)} %pad_clamp_fusion), kind=kCustom, calls=%fused_computation | custom fusion | bytes 4194336 | tf_op jit(solution)/shard_map/gather | solution.py:31
  139.2 0.8 copy.20
  139.9 0.8 pad_maximum_fusion.1
  140.7 2.6 %all-to-all-done = bf16[128,8,128]{2,0,1:T(8,128)(2,1)S(1)} async-done(((bf16[128,8,128]{2,0,1:T(8,128)(2,1)}), bf16[128,8,128]{2,0,1:T(8,128)(2,1)S(1)}, u32[]{:S(2)}, u32[]{:S(2)}) %all-to-all-start) | async-done | bytes 262176 | tf_op jit(solution)/shard_map/all_to_all | solution.py:87
  143.4 0.2 copy.17
  143.6 24.7 %reduce-scatter.2.cloned.1.call-done = f32[128,1024]{1,0:T(8,128)} async-done(((f32[1024,1024]{1,0:T(8,128)}), f32[128,1024]{1,0:T(8,128)}) %reduce-scatter.2.cloned.1.call-update) | async-done | bytes 524304 | tf_op jit(solution)/shard_map/reduce_scatter | solution.py:77
  168.3 2.0 convert_bitcast_fusion
  170.3 0.1 pad_maximum_fusion
  170.4 1.2 copy.21
  171.6 2.0 multiply_reduce_fusion
  173.6 0.7 fusion.10
  174.3 20.2 %psum.7 = f32[512]{0:T(512)S(1)} all-reduce(f32[512]{0:T(512)S(1)} %get-tuple-element.21), channel_id=1, replica_groups=mesh['pole'=2,'row'=8,'col'=2] {'row'}, use_global_device_ids=true, to_apply=%region_2.3 | all-reduce | flops 512 | bytes 4096 | tf_op jit(solution)/shard_map/psum | solution.py:111
  194.5 0.6 sub.26
  (39 shorter events, 0.3 us)
Async XLA Ops:
  7.2 0.7 copy-start
  7.2 46.4 %all-gather.2.cloned.1.call-start = ((), (), s32[]{:S(2)}) async-start(), calls=%async_computation.2 | async-start | bytes 1179648 | tf_op jit(solution)/shard_map/all_gather | solution.py:71
  9.7 158.6 %reduce-scatter.2.cloned.1.call-start = ((), (), s32[]{:S(2)}) async-start(), calls=%async_computation.3 | async-start | bytes 4718592 | tf_op jit(solution)/shard_map/reduce_scatter | solution.py:77
  60.0 0.7 copy-start.11
  60.0 1.0 copy-start.4
  60.0 1.1 copy-start.5
  60.0 47.2 %copy-start.2 = (bf16[128,1024]{1,0:T(8,128)(2,1)S(1)}, bf16[128,1024]{1,0:T(8,128)(2,1)}, u32[]{:S(2)}) copy-start(bf16[128,1024]{1,0:T(8,128)(2,1)} %param.8) | copy-start | bytes 786436
  61.2 13.3 %collective-permute-start = (bf16[256,512]{1,0:T(8,128)(2,1)S(1)}, bf16[256,512]{1,0:T(8,128)(2,1)S(1)}, u32[]{:S(2)}, u32[]{:S(2)}) collective-permute-start(bf16[256,512]{1,0:T(8,128)(2,1)S(1)} %fusion.6), channel_id=1, source_target_pairs={{0,2},{2,4},{4,6},{6,8},{8,10},{10,12},{12,14},{14,0},{1,3},{3,5},... | collective-permute-start | bytes 786440 | tf_op jit(solution)/shard_map/ppermute | solution.py:25
  74.5 16.5 %collective-permute-start.1 = (bf16[256,512]{1,0:T(8,128)(2,1)S(1)}, bf16[256,512]{1,0:T(8,128)(2,1)S(1)}, u32[]{:S(2)}, u32[]{:S(2)}) collective-permute-start(bf16[256,512]{1,0:T(8,128)(2,1)S(1)} %collective-permute-done), channel_id=1, source_target_pairs={{0,2},{2,4},{4,6},{6,8},{8,10},{10,12},{12,14},{14,0},{1,3},{3,5},... | collective-permute-start | bytes 786440 | tf_op jit(solution)/shard_map/ppermute | solution.py:25
  74.5 16.5 %collective-permute-start.4 = (bf16[256,512]{1,0:T(8,128)(2,1)S(1)}, bf16[256,512]{1,0:T(8,128)(2,1)S(1)}, u32[]{:S(2)}, u32[]{:S(2)}) collective-permute-start(bf16[256,512]{1,0:T(8,128)(2,1)S(1)} %fusion.6), channel_id=1, source_target_pairs={{2,0},{4,2},{6,4},{8,6},{10,8},{12,10},{14,12},{0,14},{3,1},{5,3},... | collective-permute-start | bytes 786440 | tf_op jit(solution)/shard_map/ppermute | solution.py:27
  91.1 16.1 %copy-start.8 = (bf16[256,512]{1,0:T(8,128)(2,1)}, bf16[256,512]{1,0:T(8,128)(2,1)S(1)}, u32[]{:S(2)}) copy-start(bf16[256,512]{1,0:T(8,128)(2,1)S(1)} %collective-permute-done.1) | copy-start | bytes 786436
  91.1 16.1 %collective-permute-start.2 = (bf16[256,512]{1,0:T(8,128)(2,1)S(1)}, bf16[256,512]{1,0:T(8,128)(2,1)S(1)}, u32[]{:S(2)}, u32[]{:S(2)}) collective-permute-start(bf16[256,512]{1,0:T(8,128)(2,1)S(1)} %collective-permute-done.1), channel_id=1, source_target_pairs={{0,2},{2,4},{4,6},{6,8},{8,10},{10,12},{12,14},{14,0},{1,3},{3,5},... | collective-permute-start | bytes 786440 | tf_op jit(solution)/shard_map/ppermute | solution.py:25
  91.1 21.1 %copy-start.6 = (bf16[256,512]{1,0:T(8,128)(2,1)}, bf16[256,512]{1,0:T(8,128)(2,1)S(1)}, u32[]{:S(2)}) copy-start(bf16[256,512]{1,0:T(8,128)(2,1)S(1)} %collective-permute-done.4) | copy-start | bytes 786436
  91.1 16.5 %collective-permute-start.5 = (bf16[256,512]{1,0:T(8,128)(2,1)S(1)}, bf16[256,512]{1,0:T(8,128)(2,1)}, u32[]{:S(2)}, u32[]{:S(2)}) collective-permute-start(bf16[256,512]{1,0:T(8,128)(2,1)S(1)} %collective-permute-done.4), channel_id=1, source_target_pairs={{2,0},{4,2},{6,4},{8,6},{10,8},{12,10},{14,12},{0,14},{3,1},{5,3},... | collective-permute-start | bytes 786440 | tf_op jit(solution)/shard_map/ppermute | solution.py:27
  107.2 5.0 %copy-start.9 = (bf16[256,512]{1,0:T(8,128)(2,1)}, bf16[256,512]{1,0:T(8,128)(2,1)S(1)}, u32[]{:S(2)}) copy-start(bf16[256,512]{1,0:T(8,128)(2,1)S(1)} %collective-permute-done.2) | copy-start | bytes 786436
  107.2 15.9 %collective-permute-start.3 = (bf16[256,512]{1,0:T(8,128)(2,1)S(1)}, bf16[256,512]{1,0:T(8,128)(2,1)}, u32[]{:S(2)}, u32[]{:S(2)}) collective-permute-start(bf16[256,512]{1,0:T(8,128)(2,1)S(1)} %collective-permute-done.2), channel_id=1, source_target_pairs={{0,2},{2,4},{4,6},{6,8},{8,10},{10,12},{12,14},{14,0},{1,3},{3,5},... | collective-permute-start | bytes 786440 | tf_op jit(solution)/shard_map/ppermute | solution.py:25
  107.6 28.6 %collective-permute-start.6 = (bf16[256,512]{1,0:T(8,128)(2,1)}, bf16[256,512]{1,0:T(8,128)(2,1)}, u32[]{:S(2)}, u32[]{:S(2)}) collective-permute-start(bf16[256,512]{1,0:T(8,128)(2,1)} %collective-permute-done.5), channel_id=1, source_target_pairs={{2,0},{4,2},{6,4},{8,6},{10,8},{12,10},{14,12},{0,14},{3,1},{5,3},... | collective-permute-start | bytes 786440 | tf_op jit(solution)/shard_map/ppermute | solution.py:27
  123.1 3.0 %copy-start.7 = (bf16[256,512]{1,0:T(8,128)(2,1)S(1)}, bf16[256,512]{1,0:T(8,128)(2,1)}, u32[]{:S(2)}) copy-start(bf16[256,512]{1,0:T(8,128)(2,1)} %copy-done.6) | copy-start | bytes 786436
  127.0 16.4 %all-to-all-start = ((bf16[128,8,128]{2,0,1:T(8,128)(2,1)}), bf16[128,8,128]{2,0,1:T(8,128)(2,1)S(1)}, u32[]{:S(2)}, u32[]{:S(2)}) async-start(bf16[128,8,128]{2,0,1:T(8,128)(2,1)} %copy.16), calls=%async_computation.1 | async-start | bytes 524288 | tf_op jit(solution)/shard_map/all_to_all | solution.py:87
  139.2 29.1 %copy-start.3 = (f32[128,1024]{1,0:T(8,128)S(1)}, f32[128,1024]{1,0:T(8,128)}, u32[]{:S(2)}) copy-start(f32[128,1024]{1,0:T(8,128)} %param.9) | copy-start | bytes 1572868
  143.6 28.0 %copy-start.1 = (bf16[8,256,512]{2,1,0:T(8,128)(2,1)S(1)}, bf16[8,256,512]{2,1,0:T(8,128)(2,1)}, u32[]{:S(2)}) copy-start(bf16[8,256,512]{2,1,0:T(8,128)(2,1)} %gather_fusion) | copy-start | bytes 6291460
  171.6 22.9 %copy-start.10 = (f32[512]{0:T(512)S(1)}, f32[512]{0:T(512)}, u32[]{:S(2)}) copy-start(f32[512]{0:T(512)} %param.15) | copy-start | bytes 6148
Sparse Core Ops, SparseCore 0:
  10.7 42.8 all-gather.1
  60.2 108.0 reduce-scatter.1
